TPU v7x, 32 devices: a whole 2x2x4 slice. The times are simulated.
32 devices in a mesh: groups: 2 (over y), col: 4 (over z), aux: 2 (over x), rep: 2 (over core).
Axes of the slice: x: 2, y: 2, z: 4, core: 2. Of those that a mesh axis runs over, the one named last changes fastest.
Arguments:
- b_aux: bfloat16 [4, 4096, 2400], P(('groups', 'aux'), ('col', 'rep')), parts along dimension 0, may hold values from -0.59765625 to 0.59765625
- occ_energies: float32 [2], P('groups'), parts along dimension 0, may hold values from -2 to -0.3
- vir_energies: float32 [4800], P('groups'), parts along dimension 0, may hold values from 0.2 to 3
- owners: int32 [2], replicated, may hold values from 0 to 7
Outputs:
- gamma: float32 [4, 4096, 2400], P(('groups', 'aux'), None, ('col', 'rep')), parts along dimension 0
There are 2 independent parts, one for each index of `groups`. A program takes and returns all parts, laid end to end along the dimension named above; an argument that names none is the same for every part. Nothing has to cross between parts.
Inputs may be any that keep to these rules, and one draw needn't show every extreme that they name: owners[s] is a column shard index in the order of col+rep; owners may repeat.
All inputs are finite; a program needn't handle non-finite values.
Results may differ from a plain program's by a relative error of at most 0.003.
Values may be sent and summed in bfloat16 or wider, within the bound.
No kernel may reach another device: no remote copies, remote signals or barrier semaphores. Data moves between devices by JAX's collectives and lax.ppermute only.
A program may use at most 64 MiB of HBM per device.

v0:
```python
import jax
import jax.numpy as jnp
from jax import lax
from jax.sharding import PartitionSpec as P

os_scale = 1.3


def from_root(value, axis, source):
    kept = jnp.where(lax.axis_index(axis) == source, value, 0).astype(value.dtype)
    return lax.psum(kept, axis)


def column_energy(first, occ_energies, vir_energies, width):
    nvirt = vir_energies.shape[0]
    occ_value = lax.dynamic_index_in_dim(occ_energies, first // nvirt, 0, keepdims=False)
    vir_values = lax.dynamic_slice_in_dim(vir_energies, first % nvirt, width, 0)
    return vir_values - occ_value


def body(b_aux, occ_energies, vir_energies, owners):
    moved = lax.all_to_all(b_aux, ("col", "rep"), split_axis=2, concat_axis=1, tiled=True)
    local_cols = moved[0]
    width = local_cols.shape[1]
    shard_index = lax.axis_index(("col", "rep"))
    energy_mine = column_energy(shard_index * width, occ_energies, vir_energies, width)
    gamma_acc = jnp.zeros(local_cols.shape, jnp.float32)
    for step_index in range(owners.shape[0]):
        owner_shard = owners[step_index]
        owner_cols = from_root(local_cols, ("col", "rep"), owner_shard)
        owner_energy = column_energy(owner_shard * width, occ_energies, vir_energies, width)
        denominator = energy_mine[:, None] + owner_energy[None, :]
        partial_value = lax.dot_general(
            local_cols, owner_cols, (((0,), (0,)), ((), ())), preferred_element_type=jnp.float32
        )
        coupling = lax.psum(partial_value, "aux")
        amplitude = (os_scale * coupling / denominator).astype(jnp.bfloat16)
        gamma_acc = gamma_acc + lax.dot_general(
            owner_cols, amplitude, (((1,), (1,)), ((), ())), preferred_element_type=jnp.float32
        )
    return gamma_acc[None]


def solution(mesh):
    placed = (P(("groups", "aux"), ("col", "rep"), None), P("groups"), P("groups"), P())
    return jax.shard_map(
        body,
        mesh=mesh,
        in_specs=placed,
        out_specs=P(("groups", "aux"), None, ("col", "rep")),
        check_vma=False,
    )
```

profile of v0, /device:TPU:0, one launch (start us, length us, event | category | flops | bytes accessed | tf_op | source)
XLA Modules:
  0.0 311.1 jit_solution(7487857900732730221)
XLA Ops:
  6.5 13.4 %copy.16 = bf16[1,512,2400]{1,0,2:T(2,128)(2,1)} copy(bf16[1,512,2400]{1,2,0:T(8,128)(2,1)} %param.4) | data formatting | bytes 4915200 | tf_op args[0]
  20.0 0.6 broadcast.16
  20.6 16.3 %reduce.2 = bf16[2400,512]{1,0:T(8,128)(2,1)S(1)} reduce(bf16[2400,1,512]{2,1,0:T(2,128)(2,1)} %bitcast.32, bf16[]{:T(256)} %broadcast.16), dimensions={1}, to_apply=%bitcast.30.reduce_sub_computation | reduce | bytes 4915202
  36.9 2.4 reshape.5
  39.3 0.0 copy-start.4
  39.3 6.5 %all-to-all-start = ((bf16[8,2,76800]{2,1,0:T(2,128)(2,1)}), bf16[8,2,76800]{2,1,0:T(2,128)(2,1)S(1)}, u32[]{:S(2)}, u32[]{:S(2)}) async-start(bf16[8,2,76800]{2,1,0:T(2,128)(2,1)} %reshape.5), calls=%async_computation | async-start | bytes 4915200 | tf_op jit(solution)/shard_map/all_to_all | solution.py:22
  45.7 0.0 all-reduce.7.cloned.1.call-start
  45.8 0.0 copy-done.4
  45.8 0.6 fusion.10
  47.7 54.8 %all-to-all-done = bf16[8,2,76800]{2,1,0:T(2,128)(2,1)S(1)} async-done(((bf16[8,2,76800]{2,1,0:T(2,128)(2,1)}), bf16[8,2,76800]{2,1,0:T(2,128)(2,1)S(1)}, u32[]{:S(2)}, u32[]{:S(2)}) %all-to-all-start) | async-done | bytes 2457632 | tf_op jit(solution)/shard_map/all_to_all | solution.py:22
  102.5 4.4 %reshape.6 = bf16[2400,1,512]{2,1,0:T(2,128)(2,1)} reshape(bf16[8,2,76800]{2,1,0:T(2,128)(2,1)S(1)} %all-to-all-done) | data formatting | bytes 4915200
  107.0 17.2 %bitcast_reduce_fusion = bf16[512,2400]{0,1:T(8,128)(2,1)} fusion(bf16[2400,1,512]{2,1,0:T(2,128)(2,1)} %reshape.6), kind=kLoop, calls=%fused_computation.22 | loop fusion | bytes 4915200 | tf_op jit(solution)/shard_map/all_to_all | solution.py:22
  124.1 2.6 all_to_all.12
  126.8 1.4 copy.15
  128.1 0.2 pad
  128.3 1.1 copy.12
  129.4 2.6 broadcast_select_fusion
  132.1 0.0 all-reduce.7.cloned.1.call-update
  132.1 0.2 all-reduce.5.cloned.1.call-start
  132.3 110.6 %all-reduce.7.cloned.1.call-done = (bf16[4096,300]{0,1:T(8,128)(2,1)}, bf16[4096,300]{0,1:T(8,128)(2,1)}) async-done(((bf16[4096,300]{0,1:T(8,128)(2,1)}, bf16[4096,300]{0,1:T(8,128)(2,1)}), (bf16[4096,300]{0,1:T(8,128)(2,1)}, bf16[4096,300]{0,1:T(8,128)(2,1)})) %all-reduce.7.cloned.1.call-update) | async-done | bytes 4915216 | tf_op jit(solution)/shard_map/psum | solution.py:11
  242.9 4.1 %convolution_bitcast_fusion.1 = f32[300,300]{0,1:T(8,128)} fusion(bf16[4096,300]{0,1:T(8,128)(2,1)} %get-tuple-element.7, bf16[4096,300]{0,1:T(8,128)(2,1)S(1)} %bitcast.34), kind=kOutput, calls=%fused_computation.6 | convolution fusion | flops 737280000 | bytes 5275200 | tf_op jit(solution)/shard_map/dot_general | solution.py:33
  247.0 0.0 copy-done
  247.0 2.3 convolution_bitcast_fusion
  249.2 0.0 all-reduce.5.cloned.1.call-update
  251.2 0.0 copy-done.3
  251.2 0.1 dynamic-slice_subtract_fusion
  251.3 35.9 %all-reduce.5.cloned.1.call-done = (f32[300,300]{0,1:T(8,128)}, f32[300,300]{0,1:T(8,128)}) async-done(((f32[300,300]{0,1:T(8,128)}, f32[300,300]{0,1:T(8,128)}), (f32[300,300]{0,1:T(8,128)}, f32[300,300]{0,1:T(8,128)})) %all-reduce.5.cloned.1.call-update) | async-done | bytes 720016 | tf_op jit(solution)/shard_map/psum | solution.py:36
  287.2 3.5 %fusion.1 = f32[4096,300]{0,1:T(8,128)S(1)} fusion(bf16[4096,300]{0,1:T(8,128)(2,1)} %get-tuple-element.7, f32[300,300]{0,1:T(8,128)} %get-tuple-element.5, f32[300]{0:T(512)S(1)} %get-tuple-element.13, f32[300]{0:T(512)S(1)} %get-tuple-element.12), kind=kOutput, calls=%fused_computation.9 | convolution fusion | flops 737640000 | bytes 7735200 | tf_op jit(solution)/shard_map/dot_general | solution.py:38
  290.7 0.0 copy-done.1
  290.7 0.0 copy-done.2
  290.7 3.9 %fusion = f32[1,4096,300]{1,2,0:T(8,128)} fusion(f32[4096,300]{0,1:T(8,128)S(1)} %fusion.1, bf16[4096,300]{0,1:T(8,128)(2,1)S(1)} %copy-done.1, f32[300,300]{0,1:T(8,128)S(1)} %copy-done.2, f32[300]{0:T(512)S(1)} %get-tuple-element.11, f32[300]{0:T(512)S(1)} %get-tuple-element.12), kind=kOutput, calls=%fused_computation.1 | convolution fusion | flops 738868800 | bytes 12650400 | tf_op jit(solution)/shard_map/dot_general | solution.py:38
  294.6 9.7 %copy.10 = f32[1,4096,300]{1,0,2:T(1,128)} copy(f32[1,4096,300]{1,2,0:T(8,128)} %fusion) | data formatting | bytes 9830400 | tf_op jit(solution)/shard_map/broadcast_in_dim | solution.py:41
  (4 shorter events, 0.0 us)
Async XLA Ops:
  39.3 6.5 %copy-start.4 = (s32[2]{0:T(128)S(1)}, s32[2]{0:T(128)}, u32[]{:S(2)}) copy-start(s32[2]{0:T(128)} %param.7) | copy-start | bytes 28
  39.3 63.2 %all-to-all-start = ((bf16[8,2,76800]{2,1,0:T(2,128)(2,1)}), bf16[8,2,76800]{2,1,0:T(2,128)(2,1)S(1)}, u32[]{:S(2)}, u32[]{:S(2)}) async-start(bf16[8,2,76800]{2,1,0:T(2,128)(2,1)} %reshape.5), calls=%async_computation | async-start | bytes 4915200 | tf_op jit(solution)/shard_map/all_to_all | solution.py:22
  45.7 197.1 %all-reduce.7.cloned.1.call-start = ((), (), s32[]{:S(2)}) async-start(), calls=%async_computation.2 | async-start | bytes 9961472 | tf_op jit(solution)/shard_map/psum | solution.py:11
  132.1 155.1 %all-reduce.5.cloned.1.call-start = ((), (), s32[]{:S(2)}) async-start(), calls=%async_computation.1 | async-start | bytes 1867776 | tf_op jit(solution)/shard_map/psum | solution.py:36
  242.9 4.1 %copy-start = (bf16[4096,300]{0,1:T(8,128)(2,1)S(1)}, bf16[4096,300]{0,1:T(8,128)(2,1)}, u32[]{:S(2)}) copy-start(bf16[4096,300]{0,1:T(8,128)(2,1)} %get-tuple-element.8) | copy-start | bytes 7372804
  247.0 4.2 %copy-start.3 = (f32[2400]{0:T(1024)S(1)}, f32[2400]{0:T(1024)}, u32[]{:S(2)}) copy-start(f32[2400]{0:T(1024)} %param.6) | copy-start | bytes 28804
  287.2 3.5 %copy-start.1 = (bf16[4096,300]{0,1:T(8,128)(2,1)S(1)}, bf16[4096,300]{0,1:T(8,128)(2,1)}, u32[]{:S(2)}) copy-start(bf16[4096,300]{0,1:T(8,128)(2,1)} %get-tuple-element.8) | copy-start | bytes 7372804
  287.2 3.5 %copy-start.2 = (f32[300,300]{0,1:T(8,128)S(1)}, f32[300,300]{0,1:T(8,128)}, u32[]{:S(2)}) copy-start(f32[300,300]{0,1:T(8,128)} %get-tuple-element.6) | copy-start | bytes 1080004
Sparse Core Ops, SparseCore 0:
  132.2 110.6 all-reduce.6
  249.4 37.7 all-reduce.4
where the time goes:
time: 312 us; the launch traced here: 311 us
  waiting for transfers between devices  201 us (64%)
  local copies, waits for them, and re-layouts  53.6 us (17%)
  other arithmetic  19.1 us (6%)
  between operations  16.7 us (5%)
  matrix products  13.7 us (4%)
  starting transfers between devices  6.72 us (2%)
    psum x1, waiting for transfers between devices, from_root(): return lax.psum(kept, axis)  111 us
    all_to_all x1, waiting for transfers between devices, body(): lax.all_to_all(b_aux, ('col', 'rep'), split_axis=2, concat_axis=1, tiled=...  54.8 us
    psum x1, waiting for transfers between devices, body(): coupling = lax.psum(partial_value, 'aux')  35.9 us
    unnamed x16, local copies, waits for them, and re-layouts  22.1 us
    all_to_all x3, local copies, waits for them, and re-layouts, body(): lax.all_to_all(b_aux, ('col', 'rep'), split_axis=2, concat_axis=1, tiled=...  21.1 us
    unnamed x1, other arithmetic  16.3 us
    broadcast_in_dim x1, local copies, waits for them, and re-layouts, body(): return gamma_acc[None]  9.71 us
    dot_general x2, matrix products, body(): lax.dot_general(owner_cols, amplitude, (((1,), (1,)), ((), ())), preferre...  7.4 us
  transfers between devices with their start and end apart: 3, of which 3 were waited for; matrix products, arithmetic and copies ran while one was open for 0% of the time, Pallas kernels for 0%

commit v1 on v0

--- a/solution.py
+++ b/solution.py
@@ -33,7 +33,8 @@
         partial_value = lax.dot_general(
             local_cols, owner_cols, (((0,), (0,)), ((), ())), preferred_element_type=jnp.float32
         )
-        coupling = lax.psum(partial_value, "aux")
+        parts = lax.all_gather(partial_value, "aux")
+        coupling = jnp.sum(parts, axis=0)
         amplitude = (os_scale * coupling / denominator).astype(jnp.bfloat16)
         gamma_acc = gamma_acc + lax.dot_general(
             owner_cols, amplitude, (((1,), (1,)), ((), ())), preferred_element_type=jnp.float32

time: 312 us -> 301 us (0.965)
  waiting for transfers between devices: 201 us -> 163 us
  blocking collectives: 0 us -> 25.6 us
  local copies, waits for them, and re-layouts: 53.6 us -> 56.9 us
    psum x1 -> x0, waiting for transfers between devices: 35.9 us -> none  [body(): coupling = lax.psum(partial_value, 'aux')]
    all_gather x0 -> x2, blocking collectives: none -> 25.6 us  [body(): parts = lax.all_gather(partial_value, 'aux')]
    unnamed x16 -> x20, local copies, waits for them, and re-layouts: 22.1 us -> 25.5 us
  transfers between devices with their start and end apart: 3 -> 2, of which waited for: 3 -> 2; matrix products, arithmetic and copies ran while one was open for 0% -> 0% of each run, Pallas kernels for 0% -> 0%
where the time goes in v1:
time: 301 us
  waiting for transfers between devices  163 us (54%)
  local copies, waits for them, and re-layouts  56.9 us (19%)
  blocking collectives  25.6 us (9%)
  other arithmetic  19.9 us (7%)
  between operations  16.7 us (6%)
  matrix products  11.4 us (4%)
  starting transfers between devices  6.67 us (2%)
    psum x1, waiting for transfers between devices, from_root(): return lax.psum(kept, axis)  109 us
    all_to_all x1, waiting for transfers between devices, body(): lax.all_to_all(b_aux, ('col', 'rep'), split_axis=2, concat_axis=1, tiled=...  54.7 us
    all_gather x2, blocking collectives, body(): parts = lax.all_gather(partial_value, 'aux')  25.6 us
    unnamed x20, local copies, waits for them, and re-layouts  25.5 us
    all_to_all x3, local copies, waits for them, and re-layouts, body(): lax.all_to_all(b_aux, ('col', 'rep'), split_axis=2, concat_axis=1, tiled=...  21.1 us
    unnamed x1, other arithmetic  16.2 us
    broadcast_in_dim x1, local copies, waits for them, and re-layouts, body(): return gamma_acc[None]  9.71 us
    dot_general x2, matrix products, body(): lax.dot_general(owner_cols, amplitude, (((1,), (1,)), ((), ())), preferre...  6.65 us
  transfers between devices with their start and end apart: 2, of which 2 were waited for; matrix products, arithmetic and copies ran while one was open for 0% of the time, Pallas kernels for 0%

profile of v1, /device:TPU:0, one launch (start us, length us, event | category | flops | bytes accessed | tf_op | source)
XLA Modules:
  0.0 300.7 jit_solution(13206882089399694322)
XLA Ops:
  6.5 13.4 %copy.22 = bf16[1,512,2400]{1,0,2:T(2,128)(2,1)} copy(bf16[1,512,2400]{1,2,0:T(8,128)(2,1)} %param.4) | data formatting | bytes 4915200 | tf_op args[0]
  20.0 0.5 broadcast.16
  20.5 16.2 %reduce.4 = bf16[2400,512]{1,0:T(8,128)(2,1)S(1)} reduce(bf16[2400,1,512]{2,1,0:T(2,128)(2,1)} %bitcast.36, bf16[]{:T(256)} %broadcast.16), dimensions={1}, to_apply=%bitcast.34.reduce_sub_computation | reduce | bytes 4915202
  36.7 2.4 reshape.13
  39.1 6.5 %all-to-all-start = ((bf16[8,2,76800]{2,1,0:T(2,128)(2,1)}), bf16[8,2,76800]{2,1,0:T(2,128)(2,1)S(1)}, u32[]{:S(2)}, u32[]{:S(2)}) async-start(bf16[8,2,76800]{2,1,0:T(2,128)(2,1)} %reshape.13), calls=%async_computation | async-start | bytes 4915200 | tf_op jit(solution)/shard_map/all_to_all | solution.py:22
  45.5 0.2 all-reduce.3.cloned.1.call-start
  45.8 0.6 fusion.10
  47.6 54.7 %all-to-all-done = bf16[8,2,76800]{2,1,0:T(2,128)(2,1)S(1)} async-done(((bf16[8,2,76800]{2,1,0:T(2,128)(2,1)}), bf16[8,2,76800]{2,1,0:T(2,128)(2,1)S(1)}, u32[]{:S(2)}, u32[]{:S(2)}) %all-to-all-start) | async-done | bytes 2457632 | tf_op jit(solution)/shard_map/all_to_all | solution.py:22
  102.3 4.4 %reshape.14 = bf16[2400,1,512]{2,1,0:T(2,128)(2,1)} reshape(bf16[8,2,76800]{2,1,0:T(2,128)(2,1)S(1)} %all-to-all-done) | data formatting | bytes 4915200
  106.8 17.1 %bitcast_reduce_fusion = bf16[512,2400]{0,1:T(8,128)(2,1)} fusion(bf16[2400,1,512]{2,1,0:T(2,128)(2,1)} %reshape.14), kind=kLoop, calls=%fused_computation.22 | loop fusion | bytes 4915200 | tf_op jit(solution)/shard_map/all_to_all | solution.py:22
  123.9 2.6 all_to_all.12
  126.5 1.4 copy.21
  127.9 0.2 pad
  128.1 1.1 copy.18
  129.2 2.6 broadcast_select_fusion
  131.8 0.0 all-reduce.3.cloned.1.call-update
  133.8 0.0 copy-done.3
  133.8 0.1 dynamic-slice_subtract_fusion
  133.9 108.7 %all-reduce.3.cloned.1.call-done = (bf16[4096,300]{0,1:T(8,128)(2,1)}, bf16[4096,300]{0,1:T(8,128)(2,1)}) async-done(((bf16[4096,300]{0,1:T(8,128)(2,1)}, bf16[4096,300]{0,1:T(8,128)(2,1)}), (bf16[4096,300]{0,1:T(8,128)(2,1)}, bf16[4096,300]{0,1:T(8,128)(2,1)})) %all-reduce.3.cloned.1.call-update) | async-done | bytes 4915216 | tf_op jit(solution)/shard_map/psum | solution.py:11
  242.6 3.3 %convolution_bitcast_fusion.1 = f32[1,300,300]{1,2,0:T(8,128)S(1)} fusion(bf16[4096,300]{0,1:T(8,128)(2,1)} %get-tuple-element.5, bf16[4096,300]{0,1:T(8,128)(2,1)S(1)} %bitcast.38), kind=kOutput, calls=%fused_computation.6 | convolution fusion | flops 737280000 | bytes 5275200 | tf_op jit(solution)/shard_map/dot_general | solution.py:33
  246.0 1.5 convolution_bitcast_fusion
  247.4 1.0 copy.12
  248.4 0.2 copy.10
  248.6 13.0 %all-gather.2 = f32[2,300,300]{2,1,0:T(8,128)S(1)} all-gather(f32[1,300,300]{2,1,0:T(8,128)S(1)} %copy.10), channel_id=2, replica_groups=mesh['groups'=2,'col'=4,'aux'=2,'rep'=2] {'aux'}, dimensions={0}, use_global_device_ids=true | all-gather | bytes 1080000 | tf_op jit(solution)/shard_map/all_gather | solution.py:36
  261.7 0.1 reduce_sum.18
  261.8 1.0 copy.16
  262.8 12.6 %all-gather.3 = f32[2,300,300]{2,1,0:T(8,128)S(1)} all-gather(f32[1,300,300]{2,1,0:T(8,128)} %copy.12), channel_id=3, replica_groups=mesh['groups'=2,'col'=4,'aux'=2,'rep'=2] {'aux'}, dimensions={0}, use_global_device_ids=true | all-gather | bytes 1080000 | tf_op jit(solution)/shard_map/all_gather | solution.py:36
  275.3 0.9 reduce_sum.19
  276.2 1.2 copy.17
  277.4 2.8 fusion.1
  280.2 3.9 %fusion = f32[1,4096,300]{1,2,0:T(8,128)} fusion(f32[4096,300]{0,1:T(8,128)S(1)} %fusion.1, bf16[4096,300]{0,1:T(8,128)(2,1)S(1)} %copy-done.1, f32[300,300]{0,1:T(8,128)S(1)} %copy.17, f32[300]{0:T(512)S(1)} %get-tuple-element.9, f32[300]{0:T(512)S(1)} %get-tuple-element.10), kind=kOutput, calls=%fused_computation.1 | convolution fusion | flops 738868800 | bytes 12650400 | tf_op jit(solution)/shard_map/dot_general | solution.py:39
  284.1 9.7 %copy.14 = f32[1,4096,300]{1,0,2:T(1,128)} copy(f32[1,4096,300]{1,2,0:T(8,128)} %fusion) | data formatting | bytes 9830400 | tf_op jit(solution)/shard_map/broadcast_in_dim | solution.py:42
  (9 shorter events, 0.0 us)
Async XLA Ops:
  39.1 6.7 %copy-start.4 = (s32[2]{0:T(128)S(1)}, s32[2]{0:T(128)}, u32[]{:S(2)}) copy-start(s32[2]{0:T(128)} %param.7) | copy-start | bytes 28
  39.1 63.2 %all-to-all-start = ((bf16[8,2,76800]{2,1,0:T(2,128)(2,1)}), bf16[8,2,76800]{2,1,0:T(2,128)(2,1)S(1)}, u32[]{:S(2)}, u32[]{:S(2)}) async-start(bf16[8,2,76800]{2,1,0:T(2,128)(2,1)} %reshape.13), calls=%async_computation | async-start | bytes 4915200 | tf_op jit(solution)/shard_map/all_to_all | solution.py:22
  45.5 197.1 %all-reduce.3.cloned.1.call-start = ((), (), s32[]{:S(2)}) async-start(), calls=%async_computation.1 | async-start | bytes 9961472 | tf_op jit(solution)/shard_map/psum | solution.py:11
  131.8 2.0 copy-start.3
  242.6 3.3 %copy-start = (bf16[4096,300]{0,1:T(8,128)(2,1)S(1)}, bf16[4096,300]{0,1:T(8,128)(2,1)}, u32[]{:S(2)}) copy-start(bf16[4096,300]{0,1:T(8,128)(2,1)} %get-tuple-element.6) | copy-start | bytes 7372804
  261.8 15.7 %copy-start.2 = (bf16[4096,300]{0,1:T(8,128)(2,1)S(1)}, bf16[4096,300]{0,1:T(8,128)(2,1)}, u32[]{:S(2)}) copy-start(bf16[4096,300]{0,1:T(8,128)(2,1)} %get-tuple-element.5) | copy-start | bytes 7372804
  277.4 2.8 copy-start.1
Sparse Core Ops, SparseCore 0:
  132.0 110.6 all-reduce.2
